TPU v7x, 256 devices: a whole 4x4x8 slice. The times are simulated.
256 devices in a mesh: row: 16 (over y, x_lo, core), col: 16 (over x_hi, z).
Axes of the slice: x: 4 (x_hi: 2, x_lo: 2; x = x_hi * 2 + x_lo), y: 4, z: 8, core: 2. Of those that a mesh axis runs over, the one named last changes fastest.
Arguments:
- w_cycle: float32 [2048, 16384], P('col', 'row'), may hold values from -0.125 to 0.125
- amps: float32 [32, 512, 2048], P('col', 'row'), may hold values from -18 to 18
- eps_occ: float32 [32], replicated, may hold values from -3 to -0.3
- eps_vir: float32 [512], replicated, may hold values from 0.3 to 3
- occ_map: int32 [4], replicated, may hold values from 0 to 31
- vir_perm: int32 [512], replicated, may hold values from 0 to 511, each once
Outputs:
- cycle: float32 [16384, 16384], P('row', 'col')
Inputs may be any that keep to these rules, and one draw needn't show every extreme that they name: `occ_map`: each window index names one occupied orbital. `vir_perm`: each virtual orbital appears once.
All inputs are finite; a program needn't handle non-finite values.
Results may differ from a plain program's by a relative error of at most 0.000071.
Values sent between devices are 32-bit elements; how exact they have to be, the bound alone decides.
No kernel may reach another device: no remote copies, remote signals or barrier semaphores. Data moves between devices by JAX's collectives and lax.ppermute only.
A program may use at most 64 MiB of HBM per device.

v0:
```python
import jax
import jax.numpy as jnp
from jax import lax
from jax.sharding import PartitionSpec as P


def lookup(indices, table):
    onehot = (indices[:, None] == jnp.arange(table.shape[0], dtype=jnp.int32)[None, :]).astype(
        jnp.float32
    )
    return jnp.dot(
        onehot, table, precision=lax.Precision.HIGHEST, preferred_element_type=jnp.float32
    )


def body(w_cycle, amps, eps_occ, eps_vir, occ_map, vir_perm):
    virtual_count = eps_vir.shape[0]
    j_local = amps.shape[0]
    b_local = amps.shape[1]
    vir_energy = lookup(vir_perm, eps_vir)
    occ_energy = lookup(occ_map, eps_occ)
    pair_energy = (vir_energy[None, :] - occ_energy[:, None]).reshape(-1)
    j_index = jnp.arange(j_local, dtype=jnp.int32) + lax.axis_index("col") * j_local
    j_energy = lookup(j_index, eps_occ)
    b_energy = lax.dynamic_slice_in_dim(vir_energy, lax.axis_index("row") * b_local, b_local)
    denominator = pair_energy[None, None, :] + b_energy[None, :, None] - j_energy[:, None, None]
    scaled = amps / denominator
    w_whole = lax.all_gather(w_cycle, "col", axis=0, tiled=True)
    regrouped = lax.all_to_all(scaled, "row", split_axis=2, concat_axis=1, tiled=True)
    t_columns = regrouped.reshape(j_local * virtual_count, regrouped.shape[2])
    return lax.dot_general(
        w_whole,
        lax.all_gather(t_columns, "row", axis=1, tiled=True),
        (((0,), (1,)), ((), ())),
        precision=lax.Precision.HIGHEST,
        preferred_element_type=jnp.float32,
    )


def solution(mesh):
    placed = (P("col", "row"), P("col", "row", None), P(), P(), P(), P())
    return jax.shard_map(
        body, mesh=mesh, in_specs=placed, out_specs=P("row", "col"), check_vma=False
    )
```

profile of v0, /device:TPU:1, one launch (start us, length us, event | category | flops | bytes accessed | tf_op | source)
XLA Modules:
  0.0 258.2 jit_solution(9936301855552644138)
XLA Ops:
  6.5 0.0 copy-start
  6.5 0.0 all-gather.5.cloned.1.call-start
  6.5 0.7 all-gather.5.cloned.1.call-update
  7.3 0.0 all-gather.3.cloned.1.call-start
  7.3 0.0 copy-done
  7.3 1.3 fusion
  8.6 0.1 dynamic_slice.3
  8.7 0.9 convolution_bitcast_fusion.2
  9.6 0.1 subtract_bitcast_fusion
  9.7 0.8 convolution_bitcast_fusion.1
  10.5 0.1 broadcast_add_fusion
  10.6 1.2 subtract_divide_fusion
  11.8 1.0 copy.17
  12.9 2.1 reshape.65
  14.9 16.8 %all_to_all.15 = f32[16,1,8192]{2,1,0:T(1,128)S(1)} all-to-all(f32[16,1,8192]{2,1,0:T(1,128)S(1)} %reshape.65), channel_id=1, replica_groups=mesh['row'=16,'col'=16] {'row'}, dimensions={0} | all-to-all | bytes 1048576 | tf_op jit(solution)/shard_map/all_to_all | solution.py:29
  31.8 0.5 broadcast.35
  32.3 1.9 reduce
  34.2 1.8 reshape.66
  36.0 2.0 copy.22
  37.9 0.0 all-gather.3.cloned.1.call-update
  38.0 113.0 %all-gather.5.cloned.1.call-done = f32[2048,1024]{1,0:T(8,128)} async-done(((f32[128,1024]{1,0:T(8,128)}), f32[2048,1024]{1,0:T(8,128)}) %all-gather.5.cloned.1.call-update) | async-done | bytes 8388624 | tf_op jit(solution)/shard_map/all_gather | solution.py:28
  150.9 63.2 %all-gather.3.cloned.1.call-done = f32[1024,2048]{1,0:T(8,128)} async-done(((f32[1024,128]{1,0:T(8,128)}), f32[1024,2048]{1,0:T(8,128)}) %all-gather.3.cloned.1.call-update) | async-done | bytes 8388624 | tf_op jit(solution)/shard_map/all_gather | solution.py:33
  214.2 31.9 %convolution_bitcast_fusion = f32[1024,1024]{0,1:T(8,128)} fusion(f32[1024,2048]{1,0:T(8,128)} %all-gather.3.cloned.1.call-done, f32[2048,1024]{1,0:T(8,128)} %all-gather.5.cloned.1.call-done), kind=kOutput, calls=%fused_computation | convolution fusion | flops 25769803776 | bytes 20971520 | tf_op jit(solution)/shard_map/dot_general | solution.py:31
  246.0 5.3 %copy.20 = f32[1024,1024]{1,0:T(8,128)} copy(f32[1024,1024]{0,1:T(8,128)} %convolution_bitcast_fusion) | data formatting | bytes 8388608 | tf_op jit(solution)/shard_map/dot_general | solution.py:31
  (2 shorter events, 0.0 us)
Async XLA Ops:
  6.5 0.8 copy-start
  6.5 144.4 %all-gather.5.cloned.1.call-start = ((), (), s32[]{:S(2)}) async-start(), calls=%async_computation.2 | async-start | bytes 8912896 | tf_op jit(solution)/shard_map/all_gather | solution.py:28
  7.3 206.9 %all-gather.3.cloned.1.call-start = ((), (), s32[]{:S(2)}) async-start(), calls=%async_computation.1 | async-start | bytes 8912896 | tf_op jit(solution)/shard_map/all_gather | solution.py:33
Sparse Core Ops, SparseCore 0:
  9.9 140.9 all-gather.4
  152.7 61.4 all-gather.2
where the time goes:
time: 258 us
  waiting for transfers between devices  177 us (69%)
  matrix products  34.9 us (14%)
  blocking collectives  16.8 us (7%)
  between operations  13.5 us (5%)
  local copies, waits for them, and re-layouts  12.8 us (5%)
  other arithmetic  3.28 us (1%)
    all_gather x1, waiting for transfers between devices, body(): w_whole = lax.all_gather(w_cycle, 'col', axis=0, tiled=True)  113 us
    all_gather x1, waiting for transfers between devices, body(): lax.all_gather(t_columns, 'row', axis=1, tiled=True)  63.2 us
    dot_general x1, matrix products, body(): lax.dot_general(w_whole, lax.all_gather(t_columns, 'row', axis=1, tiled=T...  31.9 us
    all_to_all x1, blocking collectives, body(): lax.all_to_all(scaled, 'row', split_axis=2, concat_axis=1, tiled=True)  16.8 us
    dot_general x1, local copies, waits for them, and re-layouts, body(): lax.dot_general(w_whole, lax.all_gather(t_columns, 'row', axis=1, tiled=T...  5.34 us
  transfers between devices with their start and end apart: 2, of which 2 were waited for; matrix products, arithmetic and copies ran while one was open for 5% of the time, Pallas kernels for 0%

commit v1 on v0

--- a/solution.py
+++ b/solution.py
@@ -30,7 +30,9 @@
     t_columns = regrouped.reshape(j_local * virtual_count, regrouped.shape[2])
     return lax.dot_general(
         w_whole,
-        lax.all_gather(t_columns, "row", axis=1, tiled=True),
+        jnp.concatenate(
+            lax.all_to_all(jnp.stack([t_columns] * lax.axis_size("row")), "row", 0, 0), axis=1
+        ),
         (((0,), (1,)), ((), ())),
         precision=lax.Precision.HIGHEST,
         preferred_element_type=jnp.float32,

time: 258 us -> 240 us (0.930)
  waiting for transfers between devices: 177 us -> 14.7 us
  blocking collectives: 16.8 us -> 161 us
    all_to_all x0 -> x1, blocking collectives: none -> 144 us  [body(): lax.all_to_all(jnp.stack([t_columns] * lax.axis_size('row')), 'row', 0, 0)]
    all_gather x1, waiting for transfers between devices: 113 us -> 14 us  [body(): w_whole = lax.all_gather(w_cycle, 'col', axis=0, tiled=True)]
    all_gather x1 -> x0, waiting for transfers between devices: 63.2 us -> none  [body(): lax.all_gather(t_columns, 'row', axis=1, tiled=True)]
  transfers between devices with their start and end apart: 2 -> 1, of which waited for: 2 -> 1; matrix products, arithmetic and copies ran while one was open for 5% -> 6% of each run, Pallas kernels for 0% -> 0%
where the time goes in v1:
time: 240 us
  blocking collectives  161 us (67%)
  matrix products  34.7 us (14%)
  waiting for transfers between devices  14.7 us (6%)
  between operations  13.5 us (6%)
  local copies, waits for them, and re-layouts  13 us (5%)
  other arithmetic  3.28 us (1%)
    all_to_all x1, blocking collectives, body(): lax.all_to_all(jnp.stack([t_columns] * lax.axis_size('row')), 'row', 0, 0)  144 us
    dot_general x1, matrix products, body(): lax.dot_general(w_whole, jnp.concatenate(lax.all_to_all(jnp.stack([t_colu...  31.6 us
    all_to_all x1, blocking collectives, body(): lax.all_to_all(scaled, 'row', split_axis=2, concat_axis=1, tiled=True)  16.8 us
    all_gather x1, waiting for transfers between devices, body(): w_whole = lax.all_gather(w_cycle, 'col', axis=0, tiled=True)  14 us
    dot_general x1, local copies, waits for them, and re-layouts, body(): lax.dot_general(w_whole, jnp.concatenate(lax.all_to_all(jnp.stack([t_colu...  5.34 us
  transfers between devices with their start and end apart: 1, of which 1 were waited for; matrix products, arithmetic and copies ran while one was open for 6% of the time, Pallas kernels for 0%

profile of v1, /device:TPU:1, one launch (start us, length us, event | category | flops | bytes accessed | tf_op | source)
XLA Modules:
  0.0 240.2 jit_solution(7007472429179077650)
XLA Ops:
  6.5 0.0 copy-start
  6.5 0.0 all-gather.2.cloned.1.call-start
  6.5 0.7 all-gather.2.cloned.1.call-update
  7.3 0.0 copy-done
  7.3 1.3 fusion
  8.6 0.1 dynamic_slice.3
  8.7 0.9 convolution_bitcast_fusion.2
  9.5 0.1 subtract_bitcast_fusion
  9.6 0.8 convolution_bitcast_fusion.1
  10.5 0.1 broadcast_add_fusion
  10.6 1.2 subtract_divide_fusion
  11.8 1.0 copy.20
  12.8 2.1 reshape.71
  14.9 16.8 %all_to_all.20 = f32[16,1,8192]{2,1,0:T(1,128)S(1)} all-to-all(f32[16,1,8192]{2,1,0:T(1,128)S(1)} %reshape.71), channel_id=1, replica_groups=mesh['row'=16,'col'=16] {'row'}, dimensions={0} | all-to-all | bytes 1048576 | tf_op jit(solution)/shard_map/all_to_all | solution.py:29
  31.7 0.5 broadcast.36
  32.2 1.9 reduce
  34.1 1.8 reshape.72
  35.9 0.9 copy.26
  36.8 0.2 copy.23
  37.0 1.1 stack.3
  38.1 144.3 %all_to_all.21 = f32[16,1024,128]{1,2,0:T(8,128)} all-to-all(f32[16,1024,128]{1,2,0:T(8,128)S(1)} %stack.3), channel_id=1, replica_groups=mesh['row'=16,'col'=16] {'row'}, dimensions={0} | all-to-all | bytes 16777216 | tf_op jit(solution)/shard_map/all_to_all | solution.py:34
  182.3 14.0 %all-gather.2.cloned.1.call-done = f32[2048,1024]{1,0:T(8,128)} async-done(((f32[128,1024]{1,0:T(8,128)}), f32[2048,1024]{1,0:T(8,128)}) %all-gather.2.cloned.1.call-update) | async-done | bytes 8388624 | tf_op jit(solution)/shard_map/all_gather | solution.py:28
  196.3 31.6 %convolution_bitcast_fusion = f32[1024,1024]{0,1:T(8,128)} fusion(f32[1024,2048]{0,1:T(8,128)} %bitcast.33, f32[2048,1024]{1,0:T(8,128)} %all-gather.2.cloned.1.call-done), kind=kOutput, calls=%fused_computation | convolution fusion | flops 25769803776 | bytes 20971520 | tf_op jit(solution)/shard_map/dot_general | solution.py:31
  228.0 5.3 %copy.24 = f32[1024,1024]{1,0:T(8,128)} copy(f32[1024,1024]{0,1:T(8,128)} %convolution_bitcast_fusion) | data formatting | bytes 8388608 | tf_op jit(solution)/shard_map/dot_general | solution.py:31
  (2 shorter events, 0.0 us)
Async XLA Ops:
  6.5 0.7 copy-start
  6.5 189.8 %all-gather.2.cloned.1.call-start = ((), (), s32[]{:S(2)}) async-start(), calls=%async_computation.2 | async-start | bytes 8912896 | tf_op jit(solution)/shard_map/all_gather | solution.py:28
Sparse Core Ops, SparseCore 0:
  9.9 186.3 all-gather.1

commit v2 on v0

--- a/solution.py
+++ b/solution.py
@@ -26,7 +26,10 @@
     denominator = pair_energy[None, None, :] + b_energy[None, :, None] - j_energy[:, None, None]
     scaled = amps / denominator
     w_whole = lax.all_gather(w_cycle, "col", axis=0, tiled=True)
-    regrouped = lax.all_to_all(scaled, "row", split_axis=2, concat_axis=1, tiled=True)
+    regrouped = jnp.concatenate(
+        lax.all_to_all(jnp.stack(jnp.split(scaled, lax.axis_size("row"), axis=2)), "row", 0, 0),
+        axis=1,
+    )
     t_columns = regrouped.reshape(j_local * virtual_count, regrouped.shape[2])
     return lax.dot_general(
         w_whole,

time: 258 us -> 256 us (level)
  local copies, waits for them, and re-layouts: 12.8 us -> 6.37 us
  waiting for transfers between devices: 177 us -> 183 us
    all_gather x1, waiting for transfers between devices: 113 us -> 119 us  [body(): w_whole = lax.all_gather(w_cycle, 'col', axis=0, tiled=True)]
    unnamed x5 -> x18, local copies, waits for them, and re-layouts: 3.85 us -> 0.11 us
  transfers between devices with their start and end apart: 2 -> 2, of which waited for: 2 -> 2; matrix products, arithmetic and copies ran while one was open for 5% -> 2% of each run, Pallas kernels for 0% -> 0%
where the time goes in v2:
time: 256 us; the launch traced here: 255 us
  waiting for transfers between devices  183 us (71%)
  matrix products  34.9 us (14%)
  blocking collectives  16.4 us (6%)
  between operations  13.6 us (5%)
  local copies, waits for them, and re-layouts  6.37 us (2%)
    all_gather x1, waiting for transfers between devices, body(): w_whole = lax.all_gather(w_cycle, 'col', axis=0, tiled=True)  119 us
    all_gather x1, waiting for transfers between devices, body(): lax.all_gather(t_columns, 'row', axis=1, tiled=True)  63.2 us
    dot_general x1, matrix products, body(): lax.dot_general(w_whole, lax.all_gather(t_columns, 'row', axis=1, tiled=T...  31.9 us
    all_to_all x1, blocking collectives, body(): lax.all_to_all(jnp.stack(jnp.split(scaled, lax.axis_size('row'), axis=2))...  16.4 us
    dot_general x1, local copies, waits for them, and re-layouts, body(): lax.dot_general(w_whole, lax.all_gather(t_columns, 'row', axis=1, tiled=T...  5.34 us
  transfers between devices with their start and end apart: 2, of which 2 were waited for; matrix products, arithmetic and copies ran while one was open for 2% of the time, Pallas kernels for 0%

profile of v2, /device:TPU:1, one launch (start us, length us, event | category | flops | bytes accessed | tf_op | source)
XLA Modules:
  0.0 255.4 jit_solution(11261311295360860019)
XLA Ops:
  6.5 0.0 copy-start
  6.5 0.0 all-gather.5.cloned.1.call-start
  6.5 0.7 all-gather.5.cloned.1.call-update
  7.3 0.0 all-gather.3.cloned.1.call-start
  7.3 0.0 copy-done
  7.3 1.3 fusion
  8.6 0.1 dynamic_slice.3
  8.7 0.9 convolution_bitcast_fusion.2
  9.6 0.1 subtract_bitcast_fusion
  9.7 0.8 convolution_bitcast_fusion.1
  10.5 0.1 broadcast_add_fusion
  10.6 1.2 subtract_divide_fusion
  12.1 16.4 %all_to_all.5 = f32[16,2,32,128]{3,2,1,0:T(8,128)S(1)} all-to-all(f32[16,2,32,128]{3,2,1,0:T(8,128)S(1)} %constant_dynamic-update-slice_fusion), channel_id=1, replica_groups=mesh['row'=16,'col'=16] {'row'}, dimensions={0} | all-to-all | bytes 1048576 | tf_op jit(solution)/shard_map/all_to_all | solution.py:30
  28.4 0.8 copy.24
  29.3 0.0 all-gather.3.cloned.1.call-update
  29.3 118.9 %all-gather.5.cloned.1.call-done = f32[2048,1024]{1,0:T(8,128)} async-done(((f32[128,1024]{1,0:T(8,128)}), f32[2048,1024]{1,0:T(8,128)}) %all-gather.5.cloned.1.call-update) | async-done | bytes 8388624 | tf_op jit(solution)/shard_map/all_gather | solution.py:28
  148.2 63.2 %all-gather.3.cloned.1.call-done = f32[1024,2048]{1,0:T(8,128)} async-done(((f32[1024,128]{1,0:T(8,128)}), f32[1024,2048]{1,0:T(8,128)}) %all-gather.3.cloned.1.call-update) | async-done | bytes 8388624 | tf_op jit(solution)/shard_map/all_gather | solution.py:36
  211.4 31.9 %convolution_bitcast_fusion = f32[1024,1024]{0,1:T(8,128)} fusion(f32[1024,2048]{1,0:T(8,128)} %all-gather.3.cloned.1.call-done, f32[2048,1024]{1,0:T(8,128)} %all-gather.5.cloned.1.call-done), kind=kOutput, calls=%fused_computation | convolution fusion | flops 25769803776 | bytes 20971520 | tf_op jit(solution)/shard_map/dot_general | solution.py:34
  243.3 5.3 %copy.25 = f32[1024,1024]{1,0:T(8,128)} copy(f32[1024,1024]{0,1:T(8,128)} %convolution_bitcast_fusion) | data formatting | bytes 8388608 | tf_op jit(solution)/shard_map/dot_general | solution.py:34
  (18 shorter events, 0.1 us)
Async XLA Ops:
  6.5 0.8 copy-start
  6.5 141.6 %all-gather.5.cloned.1.call-start = ((), (), s32[]{:S(2)}) async-start(), calls=%async_computation.2 | async-start | bytes 8912896 | tf_op jit(solution)/shard_map/all_gather | solution.py:28
  7.3 204.1 %all-gather.3.cloned.1.call-start = ((), (), s32[]{:S(2)}) async-start(), calls=%async_computation.1 | async-start | bytes 8912896 | tf_op jit(solution)/shard_map/all_gather | solution.py:36
Sparse Core Ops, SparseCore 0:
  9.9 138.2 all-gather.4
  149.9 61.4 all-gather.2
